TPU v7x, 128 devices: a whole 4x4x4 slice. The times are simulated.
128 devices in a mesh: seq: 32 (over x, z, y_lo), dp: 4 (over y_hi, core).
Axes of the slice: x: 4, y: 4 (y_hi: 2, y_lo: 2; y = y_hi * 2 + y_lo), z: 4, core: 2. Of those that a mesh axis runs over, the one named last changes fastest.
Arguments:
- signal: bfloat16 [65536, 128], P(('seq', 'dp')), may hold values from -6 to 6
- filter_param: bfloat16 [65536, 128], P(('seq', 'dp')), may hold values from -6 to 6
- skip_gain: float32 [128], replicated, may hold values from 0.5 to 1.5
- out_grad: bfloat16 [65536, 128], P(('seq', 'dp')), may hold values from -6 to 6
Outputs:
- conv_out: bfloat16 [65536, 128], P(('seq', 'dp'))
- input_grad: bfloat16 [65536, 128], P(('seq', 'dp'))
- filter_grad: float32 [65536, 128], P(('seq', 'dp'))
All inputs are finite; a program needn't handle non-finite values.
Results may differ from a plain program's by a relative error of at most 0.001.
Values may be sent and summed in bfloat16 or wider, within the bound.
No kernel may reach another device: no remote copies, remote signals or barrier semaphores. Data moves between devices by JAX's collectives and lax.ppermute only.
A program may use at most 64 MiB of HBM per device.

v0:
```python
import math

import jax
import jax.numpy as jnp
from jax import lax
from jax.sharding import PartitionSpec as P

FIRST_LEN = 512


highest = lax.Precision.HIGHEST


def tables(order):
    counter = jnp.arange(order, dtype=jnp.int32)
    product = counter[:, None] * counter[None, :] % order
    angle = product.astype(jnp.float32) * (2.0 * math.pi / order)
    return (jnp.cos(angle), jnp.sin(angle))


def forward_spec(stacked, dev_count, first_len):
    tok_rows, chans = stacked.shape
    first_dev = first_len // dev_count
    second_len = tok_rows // first_dev
    second_dev = second_len // dev_count
    length = first_len * second_len
    blocks = stacked.reshape(first_dev, second_len, chans)
    columns = lax.all_to_all(blocks, ("seq", "dp"), split_axis=1, concat_axis=0, tiled=True)
    cos_a, sin_a = tables(first_len)
    flat = columns.astype(jnp.float32).reshape(first_len, second_dev * chans)
    real_part = jnp.dot(cos_a, flat, precision=highest).reshape(first_len, second_dev, chans)
    imag_part = -jnp.dot(sin_a, flat, precision=highest).reshape(first_len, second_dev, chans)
    freq_idx = jnp.arange(first_len, dtype=jnp.int32)
    pos_idx = lax.axis_index(("seq", "dp")) * second_dev + jnp.arange(second_dev, dtype=jnp.int32)
    phase = (freq_idx[:, None] * pos_idx[None, :] % length).astype(jnp.float32)
    phase = (phase * (-2.0 * math.pi / length))[:, :, None]
    tw_cos = jnp.cos(phase)
    tw_sin = jnp.sin(phase)
    rot_re = real_part * tw_cos - imag_part * tw_sin
    rot_im = real_part * tw_sin + imag_part * tw_cos
    spec_re, spec_im = (
        lax.all_to_all(rot_re, ("seq", "dp"), split_axis=0, concat_axis=1, tiled=True),
        lax.all_to_all(rot_im, ("seq", "dp"), split_axis=0, concat_axis=1, tiled=True),
    )
    cos_b, sin_b = tables(second_len)
    out_re = jnp.einsum("qbc,bk->qkc", spec_re, cos_b, precision=highest) + jnp.einsum(
        "qbc,bk->qkc", spec_im, sin_b, precision=highest
    )
    out_im = jnp.einsum("qbc,bk->qkc", spec_im, cos_b, precision=highest) - jnp.einsum(
        "qbc,bk->qkc", spec_re, sin_b, precision=highest
    )
    return (columns, out_re, out_im)


def inverse_time(spec_re, spec_im, dev_count, first_len):
    first_dev, second_len, chans = spec_re.shape
    second_dev = second_len // dev_count
    length = first_len * second_len
    cos_b, sin_b = tables(second_len)
    unit_re = jnp.einsum("qkc,kb->qbc", spec_re, cos_b, precision=highest) - jnp.einsum(
        "qkc,kb->qbc", spec_im, sin_b, precision=highest
    )
    unit_im = jnp.einsum("qkc,kb->qbc", spec_im, cos_b, precision=highest) + jnp.einsum(
        "qkc,kb->qbc", spec_re, sin_b, precision=highest
    )
    freq_idx = lax.axis_index(("seq", "dp")) * first_dev + jnp.arange(first_dev, dtype=jnp.int32)
    pos_idx = jnp.arange(second_len, dtype=jnp.int32)
    phase = (freq_idx[:, None] * pos_idx[None, :] % length).astype(jnp.float32)
    phase = (phase * (2.0 * math.pi / length))[:, :, None]
    tw_cos = jnp.cos(phase)
    tw_sin = jnp.sin(phase)
    rot_re = unit_re * tw_cos - unit_im * tw_sin
    rot_im = unit_re * tw_sin + unit_im * tw_cos
    col_re, col_im = (
        lax.all_to_all(rot_re, ("seq", "dp"), split_axis=1, concat_axis=0, tiled=True),
        lax.all_to_all(rot_im, ("seq", "dp"), split_axis=1, concat_axis=0, tiled=True),
    )
    cos_a, sin_a = tables(first_len)
    flat_re = col_re.reshape(first_len, second_dev * chans)
    flat_im = col_im.reshape(first_len, second_dev * chans)
    values = jnp.dot(cos_a, flat_re, precision=highest) - jnp.dot(sin_a, flat_im, precision=highest)
    return (values * (1.0 / length)).reshape(first_len, second_dev, chans)


def per_device(signal, filter_param, skip_gain, out_grad):
    dev_count = lax.axis_size(("seq", "dp"))
    chans = skip_gain.shape[0]
    tok_rows = filter_param.shape[0]
    length = tok_rows * dev_count
    scale = 1.0 / math.sqrt(length)
    stacked = jnp.concatenate([signal, out_grad, filter_param], axis=1)
    columns, spec_re, spec_im = forward_spec(stacked, dev_count, FIRST_LEN)
    sig_re = spec_re[:, :, :chans]
    sig_im = spec_im[:, :, :chans]
    cot_re = spec_re[:, :, chans : 2 * chans]
    cot_im = spec_im[:, :, chans : 2 * chans]
    filt_re = spec_re[:, :, 2 * chans :] * scale
    filt_im = spec_im[:, :, 2 * chans :] * scale
    conv_re = sig_re * filt_re - sig_im * filt_im
    conv_im = sig_re * filt_im + sig_im * filt_re
    back_re = filt_re * cot_re + filt_im * cot_im
    back_im = filt_re * cot_im - filt_im * cot_re
    taps_re = sig_re * cot_re + sig_im * cot_im
    taps_im = sig_re * cot_im - sig_im * cot_re
    joined_re = jnp.concatenate([conv_re, back_re, taps_re], axis=2)
    joined_im = jnp.concatenate([conv_im, back_im, taps_im], axis=2)
    times = inverse_time(joined_re, joined_im, dev_count, FIRST_LEN)
    conv_cols = (
        times[:, :, :chans] + skip_gain * columns[:, :, :chans].astype(jnp.float32)
    ).astype(jnp.bfloat16)
    back_cols = (
        times[:, :, chans : 2 * chans]
        + skip_gain * columns[:, :, chans : 2 * chans].astype(jnp.float32)
    ).astype(jnp.bfloat16)
    both_rows = lax.all_to_all(
        jnp.concatenate([conv_cols, back_cols], axis=2),
        ("seq", "dp"),
        split_axis=0,
        concat_axis=1,
        tiled=True,
    )
    both_rows = both_rows.reshape(tok_rows, 2 * chans)
    conv_out = both_rows[:, :chans]
    input_grad = both_rows[:, chans:]
    taps_cols = times[:, :, 2 * chans :] * scale
    taps_rows = lax.all_to_all(taps_cols, ("seq", "dp"), split_axis=0, concat_axis=1, tiled=True)
    filter_grad = taps_rows.reshape(tok_rows, chans)
    return (conv_out, input_grad, filter_grad)


def solution(mesh):
    placed = (P(("seq", "dp"), None), P(("seq", "dp"), None), P(), P(("seq", "dp"), None))
    return jax.shard_map(
        per_device,
        mesh=mesh,
        in_specs=placed,
        out_specs=(P(("seq", "dp"), None), P(("seq", "dp"), None), P(("seq", "dp"), None)),
        check_vma=False,
    )
```

profile of v0, /device:TPU:1, one launch (start us, length us, event | category | flops | bytes accessed | tf_op | source)
XLA Modules:
  0.0 181.2 jit_solution(18326096705565502932)
XLA Ops:
  0.6 1.1 pad_maximum_fusion.6
  1.7 1.1 copy.43
  2.8 11.5 %all-to-all-start = ((bf16[4,128,384]{2,0,1:T(4,128)(2,1)}), bf16[4,128,384]{2,0,1:T(4,128)(2,1)S(1)}, u32[]{:S(2)}, u32[]{:S(2)}) async-start(bf16[4,128,384]{2,0,1:T(4,128)(2,1)} %copy.43), calls=%async_computation | async-start | bytes 786432 | tf_op jit(solution)/shard_map/all_to_all | solution.py:28
  14.3 0.1 fusion.66
  14.3 12.2 %all-to-all-done = bf16[4,128,384]{2,0,1:T(4,128)(2,1)S(1)} async-done(((bf16[4,128,384]{2,0,1:T(4,128)(2,1)}), bf16[4,128,384]{2,0,1:T(4,128)(2,1)S(1)}, u32[]{:S(2)}, u32[]{:S(2)}) %all-to-all-start) | async-done | bytes 393248 | tf_op jit(solution)/shard_map/all_to_all | solution.py:28
  26.5 0.1 reshape.148
  26.6 5.4 %convolution_negate_fusion = f32[512,384]{1,0:T(8,128)S(1)} fusion(bf16[512,384]{1,0:T(8,128)(2,1)S(1)} %reshape.148), kind=kOutput, calls=%fused_computation.12 | convolution fusion | flops 1211826176 | bytes 1179648 | tf_op jit(solution)/shard_map/dot_general | solution.py:32
  32.0 6.4 %subtract_bitcast_fusion = (f32[512,1,384]{2,0,1:T(8,128)S(1)}, f32[512,1,384]{2,0,1:T(8,128)S(1)}) fusion(f32[512,384]{1,0:T(8,128)S(1)} %convolution_negate_fusion, f32[512]{0:T(512)S(1)} %get-tuple-element.22, f32[512]{0:T(512)S(1)} %get-tuple-element.23, bf16[512,384]{1,0:T(8,128)(2,1)S(1)} %reshape.148), kind=kOutput, calls=%fused_computation.32 | convolution fusion | flops 1212809216 | bytes 2756608 | tf_op jit(solution)/shard_map/dot_general | solution.py:31
  38.4 1.7 copy.44
  40.1 4.4 %all-to-all-start.1 = ((f32[512,1,384]{2,1,0:T(1,128)}), f32[512,1,384]{2,1,0:T(1,128)S(1)}, u32[]{:S(2)}, u32[]{:S(2)}) async-start(f32[512,1,384]{2,1,0:T(1,128)} %copy.44), calls=%async_computation.1 | async-start | bytes 1572864 | tf_op jit(solution)/shard_map/all_to_all | solution.py:42
  44.5 1.7 copy.46
  46.2 14.6 %all-to-all-done.1 = f32[512,1,384]{2,1,0:T(1,128)S(1)} async-done(((f32[512,1,384]{2,1,0:T(1,128)}), f32[512,1,384]{2,1,0:T(1,128)S(1)}, u32[]{:S(2)}, u32[]{:S(2)}) %all-to-all-start.1) | async-done | bytes 786464 | tf_op jit(solution)/shard_map/all_to_all | solution.py:42
  60.8 4.7 %all-to-all-start.2 = ((f32[512,1,384]{2,1,0:T(1,128)}), f32[512,1,384]{2,1,0:T(1,128)S(1)}, u32[]{:S(2)}, u32[]{:S(2)}) async-start(f32[512,1,384]{2,1,0:T(1,128)} %copy.46), calls=%async_computation.2 | async-start | bytes 1572864 | tf_op jit(solution)/shard_map/all_to_all | solution.py:43
  65.5 0.1 fusion.65
  65.6 1.1 fusion.13
  66.7 15.1 %all-to-all-done.2 = f32[512,1,384]{2,1,0:T(1,128)S(1)} async-done(((f32[512,1,384]{2,1,0:T(1,128)}), f32[512,1,384]{2,1,0:T(1,128)S(1)}, u32[]{:S(2)}, u32[]{:S(2)}) %all-to-all-start.2) | async-done | bytes 786464 | tf_op jit(solution)/shard_map/all_to_all | solution.py:43
  81.8 1.1 fusion.15
  82.9 1.1 fusion.3
  84.0 1.1 fusion.2
  85.0 0.1 multiply_add_fusion.3
  85.1 0.2 multiply_subtract_fusion.3
  85.3 1.1 fusion.23
  86.3 1.1 fusion.22
  87.4 1.1 fusion.1
  88.5 1.2 multiply_add_fusion
  89.7 1.4 copy.49
  91.1 4.6 %all-to-all-start.4 = ((f32[4,128,384]{2,0,1:T(4,128)}), f32[4,128,384]{2,0,1:T(4,128)S(1)}, u32[]{:S(2)}, u32[]{:S(2)}) async-start(f32[4,128,384]{2,0,1:T(4,128)} %copy.49), calls=%async_computation.4 | async-start | bytes 1572864 | tf_op jit(solution)/shard_map/all_to_all | solution.py:76
  95.8 1.4 copy.48
  97.2 14.9 %all-to-all-done.4 = f32[4,128,384]{2,0,1:T(4,128)S(1)} async-done(((f32[4,128,384]{2,0,1:T(4,128)}), f32[4,128,384]{2,0,1:T(4,128)S(1)}, u32[]{:S(2)}, u32[]{:S(2)}) %all-to-all-start.4) | async-done | bytes 786464 | tf_op jit(solution)/shard_map/all_to_all | solution.py:76
  112.1 4.7 %all-to-all-start.3 = ((f32[4,128,384]{2,0,1:T(4,128)}), f32[4,128,384]{2,0,1:T(4,128)S(1)}, u32[]{:S(2)}, u32[]{:S(2)}) async-start(f32[4,128,384]{2,0,1:T(4,128)} %copy.48), calls=%async_computation.3 | async-start | bytes 1572864 | tf_op jit(solution)/shard_map/all_to_all | solution.py:75
  116.8 0.1 all_to_all.100
  116.9 0.1 copy.57
  117.0 0.1 copy.58
  117.2 0.3 reshape.150
  117.4 15.7 %all-to-all-done.3 = f32[4,128,384]{2,0,1:T(4,128)S(1)} async-done(((f32[4,128,384]{2,0,1:T(4,128)}), f32[4,128,384]{2,0,1:T(4,128)S(1)}, u32[]{:S(2)}, u32[]{:S(2)}) %all-to-all-start.3) | async-done | bytes 786464 | tf_op jit(solution)/shard_map/all_to_all | solution.py:75
  133.1 0.3 reshape.149
  133.4 6.6 %fusion.26 = f32[512,384]{0,1:T(8,128)S(1)} fusion(f32[512,384]{1,0:T(8,128)S(1)} %reshape.149), kind=kOutput, calls=%fused_computation.41 | convolution fusion | flops 1211629568 | bytes 1572864 | tf_op jit(solution)/shard_map/dot_general | solution.py:81
  140.0 0.0 copy-start
  140.0 6.7 %fusion.5 = f32[512,1,384]{0,2,1:T(8,128)S(1)} fusion(f32[512,384]{0,1:T(8,128)S(1)} %fusion.26, f32[512,384]{1,0:T(8,128)S(1)} %reshape.150), kind=kOutput, calls=%fused_computation.14 | convolution fusion | flops 1212022784 | bytes 2359296 | tf_op jit(solution)/shard_map/dot_general | solution.py:81
  146.7 0.0 copy-done
  146.8 0.1 fusion.33
  146.9 0.5 broadcast.291
  147.4 0.8 reduce.1
  148.2 0.1 copy.75
  148.4 0.9 reshape.157
  149.2 4.6 %all-to-all-start.5 = ((bf16[128,2,512]{2,1,0:T(2,128)(2,1)}), bf16[128,2,512]{2,1,0:T(2,128)(2,1)S(1)}, u32[]{:S(2)}, u32[]{:S(2)}) async-start(bf16[128,2,512]{2,1,0:T(2,128)(2,1)} %reshape.157), calls=%async_computation.5 | async-start | bytes 524288 | tf_op jit(solution)/shard_map/all_to_all | solution.py:115
  153.9 0.8 copy.54
  154.7 10.5 %all-to-all-done.5 = bf16[128,2,512]{2,1,0:T(2,128)(2,1)S(1)} async-done(((bf16[128,2,512]{2,1,0:T(2,128)(2,1)}), bf16[128,2,512]{2,1,0:T(2,128)(2,1)S(1)}, u32[]{:S(2)}, u32[]{:S(2)}) %all-to-all-start.5) | async-done | bytes 262176 | tf_op jit(solution)/shard_map/all_to_all | solution.py:115
  165.2 4.1 %all-to-all-start.6 = ((f32[512,1,128]{2,1,0:T(1,128)}), f32[512,1,128]{2,1,0:T(1,128)S(1)}, u32[]{:S(2)}, u32[]{:S(2)}) async-start(f32[512,1,128]{2,1,0:T(1,128)} %copy.54), calls=%async_computation.6 | async-start | bytes 524288 | tf_op jit(solution)/shard_map/all_to_all | solution.py:126
  169.3 0.2 reshape.158
  169.6 1.6 reduce
  171.2 0.1 all_to_all.102
  171.3 0.7 fusion.121
  172.0 8.5 %all-to-all-done.6 = f32[512,1,128]{2,1,0:T(1,128)S(1)} async-done(((f32[512,1,128]{2,1,0:T(1,128)}), f32[512,1,128]{2,1,0:T(1,128)S(1)}, u32[]{:S(2)}, u32[]{:S(2)}) %all-to-all-start.6) | async-done | bytes 262176 | tf_op jit(solution)/shard_map/all_to_all | solution.py:126
  180.5 0.7 copy.55
  (4 shorter events, 0.1 us)
Async XLA Ops:
  2.8 23.7 %all-to-all-start = ((bf16[4,128,384]{2,0,1:T(4,128)(2,1)}), bf16[4,128,384]{2,0,1:T(4,128)(2,1)S(1)}, u32[]{:S(2)}, u32[]{:S(2)}) async-start(bf16[4,128,384]{2,0,1:T(4,128)(2,1)} %copy.43), calls=%async_computation | async-start | bytes 786432 | tf_op jit(solution)/shard_map/all_to_all | solution.py:28
  40.1 20.7 %all-to-all-start.1 = ((f32[512,1,384]{2,1,0:T(1,128)}), f32[512,1,384]{2,1,0:T(1,128)S(1)}, u32[]{:S(2)}, u32[]{:S(2)}) async-start(f32[512,1,384]{2,1,0:T(1,128)} %copy.44), calls=%async_computation.1 | async-start | bytes 1572864 | tf_op jit(solution)/shard_map/all_to_all | solution.py:42
  60.8 21.0 %all-to-all-start.2 = ((f32[512,1,384]{2,1,0:T(1,128)}), f32[512,1,384]{2,1,0:T(1,128)S(1)}, u32[]{:S(2)}, u32[]{:S(2)}) async-start(f32[512,1,384]{2,1,0:T(1,128)} %copy.46), calls=%async_computation.2 | async-start | bytes 1572864 | tf_op jit(solution)/shard_map/all_to_all | solution.py:43
  91.1 21.0 %all-to-all-start.4 = ((f32[4,128,384]{2,0,1:T(4,128)}), f32[4,128,384]{2,0,1:T(4,128)S(1)}, u32[]{:S(2)}, u32[]{:S(2)}) async-start(f32[4,128,384]{2,0,1:T(4,128)} %copy.49), calls=%async_computation.4 | async-start | bytes 1572864 | tf_op jit(solution)/shard_map/all_to_all | solution.py:76
  112.1 21.0 %all-to-all-start.3 = ((f32[4,128,384]{2,0,1:T(4,128)}), f32[4,128,384]{2,0,1:T(4,128)S(1)}, u32[]{:S(2)}, u32[]{:S(2)}) async-start(f32[4,128,384]{2,0,1:T(4,128)} %copy.48), calls=%async_computation.3 | async-start | bytes 1572864 | tf_op jit(solution)/shard_map/all_to_all | solution.py:75
  140.0 6.7 %copy-start = (f32[128]{0:T(128)S(1)}, f32[128]{0:T(128)}, u32[]{:S(2)}) copy-start(f32[128]{0:T(128)} %param.6) | copy-start | bytes 1540
  149.2 15.9 %all-to-all-start.5 = ((bf16[128,2,512]{2,1,0:T(2,128)(2,1)}), bf16[128,2,512]{2,1,0:T(2,128)(2,1)S(1)}, u32[]{:S(2)}, u32[]{:S(2)}) async-start(bf16[128,2,512]{2,1,0:T(2,128)(2,1)} %reshape.157), calls=%async_computation.5 | async-start | bytes 524288 | tf_op jit(solution)/shard_map/all_to_all | solution.py:115
  165.2 15.3 %all-to-all-start.6 = ((f32[512,1,128]{2,1,0:T(1,128)}), f32[512,1,128]{2,1,0:T(1,128)S(1)}, u32[]{:S(2)}, u32[]{:S(2)}) async-start(f32[512,1,128]{2,1,0:T(1,128)} %copy.54), calls=%async_computation.6 | async-start | bytes 524288 | tf_op jit(solution)/shard_map/all_to_all | solution.py:126
where the time goes:
time: 182 us; the launch traced here: 181 us
  waiting for transfers between devices  91.6 us (50%)
  starting transfers between devices  38.6 us (21%)
  matrix products  33.7 us (19%)
  local copies, waits for them, and re-layouts  12.4 us (7%)
  other arithmetic  4 us (2%)
    all_to_all x1, waiting for transfers between devices, inverse_time(): lax.all_to_all(rot_re, ('seq', 'dp'), split_axis=1, concat_axis=0, tiled=...  15.7 us
    all_to_all x1, waiting for transfers between devices, forward_spec(): lax.all_to_all(rot_im, ('seq', 'dp'), split_axis=0, concat_axis=1, tiled=...  15.1 us
    all_to_all x1, waiting for transfers between devices, inverse_time(): lax.all_to_all(rot_im, ('seq', 'dp'), split_axis=1, concat_axis=0, tiled=...  14.9 us
    all_to_all x1, waiting for transfers between devices, forward_spec(): lax.all_to_all(rot_re, ('seq', 'dp'), split_axis=0, concat_axis=1, tiled=...  14.6 us
    all_to_all x1, waiting for transfers between devices, forward_spec(): lax.all_to_all(blocks, ('seq', 'dp'), split_axis=1, concat_axis=0, tiled=...  12.2 us
    all_to_all x1, starting transfers between devices, forward_spec(): lax.all_to_all(blocks, ('seq', 'dp'), split_axis=1, concat_axis=0, tiled=...  11.5 us
    all_to_all x1, waiting for transfers between devices, per_device(): lax.all_to_all(jnp.concatenate([conv_cols, back_cols], axis=2), ('seq', '...  10.5 us
    all_to_all x1, waiting for transfers between devices, per_device(): lax.all_to_all(taps_cols, ('seq', 'dp'), split_axis=0, concat_axis=1, til...  8.55 us
  transfers between devices with their start and end apart: 7, of which 7 were waited for; matrix products, arithmetic and copies ran while one was open for 5% of the time, Pallas kernels for 0%

commit v1 on v0

v1 whole, which is shorter than its diff:
```python
import math

import numpy as np

import jax
import jax.numpy as jnp
from jax import lax
from jax.sharding import PartitionSpec as P

FIRST_LEN = 512
AXES = ("seq", "dp")

highest = lax.Precision.HIGHEST


def half_table(order):
    half = order // 2
    slot = np.arange(half)[:, None]
    pos = np.arange(order)[None, :]
    angle = (slot * pos % order) * (2.0 * np.pi / order)
    real_rows = np.cos(angle)
    imag_rows = -np.sin(angle)
    real_rows[0, :] = 1.0
    imag_rows[0, :] = np.where(np.arange(order) % 2 == 0, 1.0, -1.0)
    return jnp.asarray(np.concatenate([real_rows, imag_rows], axis=0), dtype=jnp.float32)


def full_table(order):
    idx = np.arange(order)
    angle = (idx[:, None] * idx[None, :] % order) * (2.0 * np.pi / order)
    c, s = np.cos(angle), np.sin(angle)
    top = np.concatenate([c, s], axis=1)
    bottom = np.concatenate([-s, c], axis=1)
    return jnp.asarray(np.concatenate([top, bottom], axis=0), dtype=jnp.float32)


def rotate(re, im, cos_t, sin_t):
    return re * cos_t - im * sin_t, re * sin_t + im * cos_t


def per_device(signal, filter_param, skip_gain, out_grad):
    dev_count = lax.axis_size(AXES)
    me = lax.axis_index(AXES)
    tok_rows, chans = signal.shape
    length = tok_rows * dev_count
    first_len = FIRST_LEN
    second_len = length // first_len
    first_dev = first_len // dev_count
    half = first_len // 2
    slots = half // dev_count
    assert second_len == dev_count and slots * dev_count == half

    stacked = jnp.concatenate([signal, out_grad, filter_param], axis=1)
    blocks = stacked.reshape(first_dev, second_len, 3 * chans)
    columns = lax.all_to_all(blocks, AXES, split_axis=1, concat_axis=0, tiled=True)
    columns = columns.reshape(first_len, 3 * chans).astype(jnp.float32)

    table_a = half_table(first_len)
    part = jnp.dot(table_a, columns, precision=highest)
    part = part.reshape(2, dev_count, slots, 3 * chans)

    got = lax.all_to_all(part, AXES, split_axis=1, concat_axis=1, tiled=True)
    z_re, z_im = got[0], got[1]

    pos_b = jnp.arange(second_len, dtype=jnp.float32)[:, None]
    freq = (me * slots + jnp.arange(slots, dtype=jnp.int32)).astype(jnp.float32)[None, :]
    phase = pos_b * freq * (-2.0 * math.pi / length)
    tw_c = jnp.cos(phase)[:, :, None]
    tw_s = jnp.sin(phase)[:, :, None]
    t_re, t_im = rotate(z_re, z_im, tw_c, tw_s)
    is_first = me == 0
    t_im0 = jnp.where(is_first, 0.0, t_im[:, 0:1])
    nyq_phase = pos_b * (-2.0 * math.pi * half / length)
    nyq_c = jnp.cos(nyq_phase)[:, :, None]
    nyq_s = jnp.sin(nyq_phase)[:, :, None]
    extra_re = jnp.where(is_first, z_im[:, 0:1] * nyq_c, 0.0)
    extra_im = jnp.where(is_first, z_im[:, 0:1] * nyq_s, 0.0)
    rows_re = jnp.concatenate([t_re, extra_re], axis=1)
    rows_im = jnp.concatenate([t_im0, t_im[:, 1:], extra_im], axis=1)
    nrows = slots + 1

    table_b = full_table(second_len)
    both = jnp.stack([rows_re, rows_im]).reshape(2 * second_len, nrows * 3 * chans)
    spec = jnp.dot(table_b, both, precision=highest).reshape(2, second_len, nrows, 3 * chans)
    sr, si = spec[0], spec[1]
    sig_r, cot_r, flt_r = sr[..., :chans], sr[..., chans : 2 * chans], sr[..., 2 * chans :]
    sig_i, cot_i, flt_i = si[..., :chans], si[..., chans : 2 * chans], si[..., 2 * chans :]

    scale = 1.0 / (math.sqrt(length) * length)
    conv_r = (sig_r * flt_r - sig_i * flt_i) * scale
    conv_i = (sig_r * flt_i + sig_i * flt_r) * scale
    back_r = (flt_r * cot_r + flt_i * cot_i) * scale
    back_i = (flt_r * cot_i - flt_i * cot_r) * scale
    taps_r = (sig_r * cot_r + sig_i * cot_i) * scale
    taps_i = (sig_r * cot_i - sig_i * cot_r) * scale
    prod = jnp.stack(
        [
            jnp.concatenate([conv_r, back_r, taps_r], axis=-1),
            jnp.concatenate([conv_i, back_i, taps_i], axis=-1),
        ]
    ).reshape(2 * second_len, nrows * 3 * chans)

    unit = lax.dot_general(
        table_b, prod, (((0,), (0,)), ((), ())), precision=highest
    ).reshape(2, second_len, nrows, 3 * chans)
    u_re, u_im = unit[0], unit[1]
    v_re, v_im = rotate(u_re[:, :slots], u_im[:, :slots], tw_c, -tw_s)
    x_re, _ = rotate(u_re[:, slots:], u_im[:, slots:], nyq_c, -nyq_s)
    out_re0 = jnp.where(is_first, v_re[:, 0:1], 2.0 * v_re[:, 0:1])
    out_im0 = jnp.where(is_first, x_re, 2.0 * v_im[:, 0:1])
    out_re = jnp.concatenate([out_re0, 2.0 * v_re[:, 1:]], axis=1)
    out_im = jnp.concatenate([out_im0, 2.0 * v_im[:, 1:]], axis=1)
    back_part = jnp.stack([out_re, out_im])

    ret = lax.all_to_all(back_part, AXES, split_axis=1, concat_axis=1, tiled=True)
    ret = ret.reshape(first_len, 3 * chans)

    times = lax.dot_general(table_a, ret, (((0,), (0,)), ((), ())), precision=highest)
    conv_cols = times[:, :chans] + skip_gain * columns[:, :chans]
    back_cols = times[:, chans : 2 * chans] + skip_gain * columns[:, chans : 2 * chans]
    taps_cols = times[:, 2 * chans :]
    taps_hi = lax.reduce_precision(taps_cols, exponent_bits=8, mantissa_bits=7)
    taps_lo = taps_cols - taps_hi
    outs = jnp.concatenate(
        [
            conv_cols.astype(jnp.bfloat16),
            back_cols.astype(jnp.bfloat16),
            taps_hi.astype(jnp.bfloat16),
            taps_lo.astype(jnp.bfloat16),
        ],
        axis=1,
    ).reshape(dev_count, first_dev, 1, 4 * chans)

    rows = lax.all_to_all(outs, AXES, split_axis=0, concat_axis=2, tiled=True)
    rows = rows.reshape(tok_rows, 4 * chans)
    conv_out = rows[:, :chans]
    input_grad = rows[:, chans : 2 * chans]
    filter_grad = rows[:, 2 * chans : 3 * chans].astype(jnp.float32) + rows[:, 3 * chans :].astype(
        jnp.float32
    )
    return (conv_out, input_grad, filter_grad)


def solution(mesh):
    placed = (P(AXES, None), P(AXES, None), P(), P(AXES, None))
    return jax.shard_map(
        per_device,
        mesh=mesh,
        in_specs=placed,
        out_specs=(P(AXES, None), P(AXES, None), P(AXES, None)),
        check_vma=False,
    )
```

time: 182 us -> 103 us (0.57)
  waiting for transfers between devices: 91.6 us -> 31.7 us
  blocking collectives: 0 us -> 41.2 us
  starting transfers between devices: 38.6 us -> 9.18 us
  matrix products: 33.7 us -> 5.95 us
  local copies, waits for them, and re-layouts: 12.4 us -> 9.97 us
    all_to_all x7 -> x2, waiting for transfers between devices: 91.6 us -> 31.7 us  [the longest x1 16.1 us: per_device(): got = lax.all_to_all(part, AXES, split_axis=1, concat_axis=1, tiled=True)]
    all_to_all x0 -> x2, blocking collectives: none -> 41.2 us  [the longest x1 23.5 us: per_device(): lax.all_to_all(blocks, AXES, split_axis=1, concat_axis=0, tiled=True)]
    all_to_all x7 -> x2, starting transfers between devices: 38.6 us -> 9.18 us  [the longest x1 4.83 us: per_device(): lax.all_to_all(back_part, AXES, split_axis=1, concat_axis=1, tiled=True)]
    dot_general x12 -> x4, matrix products: 33.7 us -> 5.95 us  [the longest x1 2.23 us: per_device(): lax.dot_general(table_b, prod, (((0,), (0,)), ((), ())), precision=highest)]
    add x2 -> x0, local copies, waits for them, and re-layouts: 3.12 us -> none  [the longest x1 1.7 us: forward_spec(): rot_im = real_part * tw_sin + imag_part * tw_cos]
    sub x2 -> x0, local copies, waits for them, and re-layouts: 3.12 us -> none  [the longest x1 1.72 us: forward_spec(): rot_re = real_part * tw_cos - imag_part * tw_sin]
    another operation x0 -> x3, local copies, waits for them, and re-layouts: none -> 3.03 us  [the longest x1 1.2 us: per_device(): back_part = jnp.stack([out_re, out_im])]
  transfers between devices with their start and end apart: 7 -> 2, of which waited for: 7 -> 2; matrix products, arithmetic and copies ran while one was open for 5% -> 1% of each run, Pallas kernels for 0% -> 0%
where the time goes in v1:
time: 103 us; the launch traced here: 102 us
  blocking collectives  41.2 us (40%)
  waiting for transfers between devices  31.7 us (31%)
  local copies, waits for them, and re-layouts  9.97 us (10%)
  starting transfers between devices  9.18 us (9%)
  matrix products  5.95 us (6%)
  other arithmetic  3.32 us (3%)
    all_to_all x1, blocking collectives, per_device(): lax.all_to_all(blocks, AXES, split_axis=1, concat_axis=0, tiled=True)  23.5 us
    all_to_all x1, blocking collectives, per_device(): rows = lax.all_to_all(outs, AXES, split_axis=0, concat_axis=2, tiled=True)  17.6 us
    all_to_all x1, waiting for transfers between devices, per_device(): got = lax.all_to_all(part, AXES, split_axis=1, concat_axis=1, tiled=True)  16.1 us
    all_to_all x1, waiting for transfers between devices, per_device(): lax.all_to_all(back_part, AXES, split_axis=1, concat_axis=1, tiled=True)  15.6 us
    all_to_all x1, starting transfers between devices, per_device(): lax.all_to_all(back_part, AXES, split_axis=1, concat_axis=1, tiled=True)  4.83 us
    all_to_all x1, starting transfers between devices, per_device(): got = lax.all_to_all(part, AXES, split_axis=1, concat_axis=1, tiled=True)  4.36 us
    dot_general x1, matrix products, per_device(): lax.dot_general(table_b, prod, (((0,), (0,)), ((), ())), precision=highest)  2.23 us
  transfers between devices with their start and end apart: 2, of which 2 were waited for; matrix products, arithmetic and copies ran while one was open for 1% of the time, Pallas kernels for 0%

profile of v1, /device:TPU:1, one launch (start us, length us, event | category | flops | bytes accessed | tf_op | source)
XLA Modules:
  0.0 102.3 jit_solution(3189238744467558587)
XLA Ops:
  0.6 1.1 %pad_maximum_fusion.4 = bf16[512,384]{1,0:T(8,128)(2,1)S(1)} fusion(bf16[512,128]{1,0:T(8,128)(2,1)} %param.7, bf16[512,128]{1,0:T(8,128)(2,1)} %param.9, bf16[512,128]{1,0:T(8,128)(2,1)} %param.6), kind=kLoop, calls=%fused_computation.15 | loop fusion | flops 1179648 | bytes 786432 | tf_op jit(solution)/shard_map/concatenate | solution.py:53
  1.7 0.0 copy-start.2
  1.7 0.3 copy.52
  2.0 23.5 %all_to_all.40 = bf16[4,128,384]{2,0,1:T(4,128)(2,1)S(1)} all-to-all(bf16[4,128,384]{2,0,1:T(4,128)(2,1)S(1)} %copy.52), channel_id=1, replica_groups=mesh['seq'=32,'dp'=4] {'seq','dp'}, dimensions={1} | all-to-all | bytes 786432 | tf_op jit(solution)/shard_map/all_to_all | solution.py:55
  25.6 0.0 copy-done.2
  25.6 1.0 fusion.24
  26.6 0.5 reshape.132
  27.1 1.1 %copy.54 = f32[2,128,2,384]{3,2,0,1:T(2,128)} copy(f32[2,128,2,384]{3,2,1,0:T(2,128)S(1)} %reshape.132) | data formatting | bytes 1572864 | tf_op jit(solution)/shard_map/reshape | solution.py:60
  28.3 4.4 %all-to-all-start.1 = ((f32[2,128,2,384]{3,2,0,1:T(2,128)}), f32[2,128,2,384]{3,2,0,1:T(2,128)S(1)}, u32[]{:S(2)}, u32[]{:S(2)}) async-start(f32[2,128,2,384]{3,2,0,1:T(2,128)} %copy.54), calls=%async_computation.1 | async-start | bytes 1572864 | tf_op jit(solution)/shard_map/all_to_all | solution.py:62
  32.8 0.1 fusion.18
  32.9 16.1 %all-to-all-done.1 = f32[2,128,2,384]{3,2,0,1:T(2,128)S(1)} async-done(((f32[2,128,2,384]{3,2,0,1:T(2,128)}), f32[2,128,2,384]{3,2,0,1:T(2,128)S(1)}, u32[]{:S(2)}, u32[]{:S(2)}) %all-to-all-start.1) | async-done | bytes 786464 | tf_op jit(solution)/shard_map/all_to_all | solution.py:62
  49.0 0.3 fusion.22
  49.2 0.2 copy.71
  49.4 0.2 copy.70
  49.6 0.1 fusion.6
  49.8 0.1 maximum_bitcast_fusion
  49.9 0.1 maximum_bitcast_fusion.1
  49.9 0.1 pad_maximum_fusion
  50.0 0.0 copy-start
  50.0 0.9 copy.57
  51.0 0.0 copy-done
  51.0 1.3 %fusion.3 = f32[256,1152]{1,0:T(8,128)S(1)} fusion(f32[256,256]{1,0:T(8,128)S(1)} %copy-done, f32[144,8,2,128]{3,2,1,0:T(2,128)S(1)} %bitcast.66), kind=kOutput, calls=%fused_computation.3 | convolution fusion | flops 905969664 | bytes 2621440 | tf_op jit(solution)/shard_map/dot_general | solution.py:84
  52.2 0.1 fusion.20
  52.3 0.2 copy.58
  52.6 0.2 copy.59
  52.8 0.1 add_multiply_fusion.2
  52.9 0.1 subtract_multiply_fusion.2
  53.1 0.1 pad_maximum_fusion.1
  53.2 0.9 copy.60
  54.1 2.2 %fusion = f32[256,1152]{1,0:T(8,128)S(1)} fusion(f32[256,256]{1,0:T(8,128)S(1)} %copy-done, f32[144,8,2,128]{3,2,1,0:T(2,128)S(1)} %bitcast.65), kind=kOutput, calls=%fused_computation | convolution fusion | flops 905969664 | bytes 2621440 | tf_op jit(solution)/shard_map/dot_general | solution.py:103
  56.3 0.1 fusion.19
  56.4 0.2 copy.61
  56.6 0.2 copy.62
  56.9 0.1 multiply_subtract_fusion
  57.0 0.1 multiply_select_fusion
  57.1 0.1 pad_maximum_fusion.2
  57.2 1.2 %copy.63 = f32[2,128,2,384]{3,2,0,1:T(2,128)} copy(f32[2,128,2,384]{1,3,2,0:T(8,128)S(1)} %pad_maximum_fusion.2) | data formatting | bytes 1572864 | tf_op jit(solution)/shard_map/stack | solution.py:113
  58.4 4.8 %all-to-all-start.2 = ((f32[2,128,2,384]{3,2,0,1:T(2,128)}), f32[2,128,2,384]{3,2,0,1:T(2,128)S(1)}, u32[]{:S(2)}, u32[]{:S(2)}) async-start(f32[2,128,2,384]{3,2,0,1:T(2,128)} %copy.63), calls=%async_computation.2 | async-start | bytes 1572864 | tf_op jit(solution)/shard_map/all_to_all | solution.py:115
  63.3 0.1 convert_bitcast_fusion
  63.4 0.3 reshape.142
  63.7 0.1 copy.72
  63.8 0.1 copy.73
  64.0 15.6 %all-to-all-done.2 = f32[2,128,2,384]{3,2,0,1:T(2,128)S(1)} async-done(((f32[2,128,2,384]{3,2,0,1:T(2,128)}), f32[2,128,2,384]{3,2,0,1:T(2,128)S(1)}, u32[]{:S(2)}, u32[]{:S(2)}) %all-to-all-start.2) | async-done | bytes 786464 | tf_op jit(solution)/shard_map/all_to_all | solution.py:115
  79.6 0.3 copy.64
  79.9 0.0 copy-start.1
  79.9 0.5 reshape.135
  80.4 0.7 copy-done.1
  81.1 0.0 copy-start.3
  81.1 1.5 %fusion.25 = f32[512,384]{0,1:T(8,128)S(1)} fusion(f32[512,512]{1,0:T(8,128)S(1)} %copy-done.1, f32[512,384]{1,0:T(8,128)S(1)} %reshape.135), kind=kOutput, calls=%fused_computation.64 | convolution fusion | flops 1207959552 | bytes 2621440 | tf_op jit(solution)/shard_map/dot_general | solution.py:118
  82.6 0.0 copy-done.3
  82.6 0.1 fusion.10
  82.8 0.2 copy.67
  83.0 0.1 reshape.136
  83.1 17.6 %all_to_all.41 = bf16[128,4,1,512]{3,1,2,0:T(4,128)(2,1)S(1)} all-to-all(bf16[128,4,1,512]{3,1,2,0:T(4,128)(2,1)S(1)} %bitcast.74), channel_id=1, replica_groups=mesh['seq'=32,'dp'=4] {'seq','dp'}, dimensions={0} | all-to-all | bytes 1048576 | tf_op jit(solution)/shard_map/all_to_all | solution.py:134
  100.7 0.1 copy.69
  100.8 0.7 fusion.23
  101.6 0.7 convert_add_fusion
  (13 shorter events, 0.5 us)
Async XLA Ops:
  1.7 23.9 %copy-start.2 = (f32[512,512]{1,0:T(8,128)S(1)}, f32[512,512]{1,0:T(8,128)}, u32[]{:S(2)}) copy-start(f32[512,512]{1,0:T(8,128)} %constant.33) | copy-start | bytes 3145732
  28.3 20.7 %all-to-all-start.1 = ((f32[2,128,2,384]{3,2,0,1:T(2,128)}), f32[2,128,2,384]{3,2,0,1:T(2,128)S(1)}, u32[]{:S(2)}, u32[]{:S(2)}) async-start(f32[2,128,2,384]{3,2,0,1:T(2,128)} %copy.54), calls=%async_computation.1 | async-start | bytes 1572864 | tf_op jit(solution)/shard_map/all_to_all | solution.py:62
  50.0 1.0 copy-start
  58.4 21.2 %all-to-all-start.2 = ((f32[2,128,2,384]{3,2,0,1:T(2,128)}), f32[2,128,2,384]{3,2,0,1:T(2,128)S(1)}, u32[]{:S(2)}, u32[]{:S(2)}) async-start(f32[2,128,2,384]{3,2,0,1:T(2,128)} %copy.63), calls=%async_computation.2 | async-start | bytes 1572864 | tf_op jit(solution)/shard_map/all_to_all | solution.py:115
  79.9 1.2 %copy-start.1 = (f32[512,512]{1,0:T(8,128)S(1)}, f32[512,512]{1,0:T(8,128)}, u32[]{:S(2)}) copy-start(f32[512,512]{1,0:T(8,128)} %constant.29.clone) | copy-start | bytes 3145732
  81.1 1.5 %copy-start.3 = (f32[128]{0:T(128)S(1)}, f32[128]{0:T(128)}, u32[]{:S(2)}) copy-start(f32[128]{0:T(128)} %param.8) | copy-start | bytes 1540

commit v2 on v1

v2 whole, which is shorter than its diff:
```python
import math

import numpy as np

import jax
import jax.numpy as jnp
from jax import lax
from jax.sharding import PartitionSpec as P

AXES = ("seq", "dp")

highest = lax.Precision.HIGHEST


def half_table(order):
    half = order // 2
    slot = np.arange(half)[:, None]
    pos = np.arange(order)[None, :]
    angle = (slot * pos % order) * (2.0 * np.pi / order)
    real_rows = np.cos(angle)
    imag_rows = -np.sin(angle)
    real_rows[0, :] = 1.0
    imag_rows[0, :] = np.where(np.arange(order) % 2 == 0, 1.0, -1.0)
    return jnp.asarray(np.concatenate([real_rows, imag_rows], axis=0), dtype=jnp.float32)


def pair_table(order):
    idx = np.arange(order)
    angle = (idx[:, None] * idx[None, :] % order) * (2.0 * np.pi / order)
    return jnp.asarray(np.concatenate([np.cos(angle), np.sin(angle)], axis=1), dtype=jnp.float32)


def twiddle(rows, cols, length):
    k = np.arange(rows)[:, None]
    n = np.arange(cols)[None, :]
    angle = (k * n % length) * (-2.0 * np.pi / length)
    return (
        jnp.asarray(np.cos(angle), dtype=jnp.float32),
        jnp.asarray(np.sin(angle), dtype=jnp.float32),
    )


def rotate(re, im, cos_t, sin_t):
    return re * cos_t - im * sin_t, re * sin_t + im * cos_t


def per_device(signal, filter_param, skip_gain, out_grad):
    dev_count = lax.axis_size(AXES)
    me = lax.axis_index(AXES)
    tok_rows, chans = signal.shape
    length = tok_rows * dev_count
    side = math.isqrt(length)
    half = side // 2
    assert chans == dev_count and side * side == length

    stacked = jnp.stack([signal, out_grad, filter_param], axis=0)
    send = jnp.transpose(stacked, (2, 0, 1))
    got = lax.all_to_all(send, AXES, split_axis=0, concat_axis=2, tiled=True)
    seqs = got.reshape(3, side, side).astype(jnp.float32)

    table_a = half_table(side)
    part = jnp.einsum("kn,anm->akm", table_a, seqs, precision=highest)
    y_re, y_im = part[:, :half], part[:, half:]
    zero_row = jnp.zeros((3, 1, side), jnp.float32)
    rows_re = jnp.concatenate([y_re, y_im[:, 0:1]], axis=1)
    rows_im = jnp.concatenate([zero_row, y_im[:, 1:], zero_row], axis=1)
    tw_c, tw_s = twiddle(half + 1, side, length)
    t_re, t_im = rotate(rows_re, rows_im, tw_c, tw_s)

    table_b = pair_table(side)
    both = jnp.concatenate([t_re, t_im], axis=0)
    prod_b = jnp.einsum("akn,nm->akm", both, table_b, precision=highest)
    cc, cs = prod_b[..., :side], prod_b[..., side:]
    s_re = cc[:3] + cs[3:]
    s_im = cc[3:] - cs[:3]
    sig_r, cot_r, flt_r = s_re[0], s_re[1], s_re[2]
    sig_i, cot_i, flt_i = s_im[0], s_im[1], s_im[2]

    scale = 1.0 / (math.sqrt(length) * length)
    p_re = jnp.stack(
        [
            sig_r * flt_r - sig_i * flt_i,
            flt_r * cot_r + flt_i * cot_i,
            sig_r * cot_r + sig_i * cot_i,
        ]
    ) * scale
    p_im = jnp.stack(
        [
            sig_r * flt_i + sig_i * flt_r,
            flt_r * cot_i - flt_i * cot_r,
            sig_r * cot_i - sig_i * cot_r,
        ]
    ) * scale

    both = jnp.concatenate([p_re, p_im], axis=0)
    prod_b = jnp.einsum("akn,nm->akm", both, table_b, precision=highest)
    cc, cs = prod_b[..., :side], prod_b[..., side:]
    u_re = cc[:3] - cs[3:]
    u_im = cc[3:] + cs[:3]
    v_re, v_im = rotate(u_re, u_im, tw_c, -tw_s)

    pack_re = jnp.concatenate([v_re[:, 0:1], 2.0 * v_re[:, 1:half]], axis=1)
    pack_im = jnp.concatenate([v_re[:, half:], 2.0 * v_im[:, 1:half]], axis=1)
    packed = jnp.concatenate([pack_re, pack_im], axis=1)
    times = jnp.einsum("sn,asm->anm", table_a, packed, precision=highest).reshape(3, length)

    gain = lax.dynamic_index_in_dim(skip_gain, me, keepdims=False)
    flat = seqs.reshape(3, length)
    conv = times[0] + gain * flat[0]
    back = times[1] + gain * flat[1]
    taps = times[2]
    taps_hi = lax.reduce_precision(taps, exponent_bits=8, mantissa_bits=7)
    taps_lo = taps - taps_hi
    outs = jnp.stack(
        [
            conv.astype(jnp.bfloat16),
            back.astype(jnp.bfloat16),
            taps_hi.astype(jnp.bfloat16),
            taps_lo.astype(jnp.bfloat16),
        ]
    ).reshape(4, dev_count, tok_rows)

    rows = lax.all_to_all(outs, AXES, split_axis=1, concat_axis=1, tiled=True)
    rows = jnp.transpose(rows, (0, 2, 1))
    conv_out = rows[0]
    input_grad = rows[1]
    filter_grad = rows[2].astype(jnp.float32) + rows[3].astype(jnp.float32)
    return (conv_out, input_grad, filter_grad)


def solution(mesh):
    placed = (P(AXES, None), P(AXES, None), P(), P(AXES, None))
    return jax.shard_map(
        per_device,
        mesh=mesh,
        in_specs=placed,
        out_specs=(P(AXES, None), P(AXES, None), P(AXES, None)),
        check_vma=False,
    )
```

time: 103 us -> 55.7 us (0.54)
  blocking collectives: 41.2 us -> 17.6 us
  waiting for transfers between devices: 31.7 us -> 12.8 us
  local copies, waits for them, and re-layouts: 9.97 us -> 4.68 us
  starting transfers between devices: 9.18 us -> 11.5 us
  matrix products: 5.95 us -> 4.43 us
    all_to_all x2 -> x1, blocking collectives: 41.2 us -> 17.6 us  [per_device(): rows = lax.all_to_all(outs, AXES, split_axis=1, concat_axis=1, tiled=True)]
    all_to_all x2 -> x1, waiting for transfers between devices: 31.7 us -> 12.8 us  [per_device(): got = lax.all_to_all(send, AXES, split_axis=0, concat_axis=2, tiled=True)]
    another operation x3 -> x1, local copies, waits for them, and re-layouts: 3.03 us -> 0.41 us  [per_device(): jnp.stack([conv.astype(jnp.bfloat16), back.astype(jnp.bfloat16), taps_hi....]
    reshape x5 -> x1, local copies, waits for them, and re-layouts: 2.58 us -> 0.13 us  [per_device(): seqs = got.reshape(3, side, side).astype(jnp.float32)]
    all_to_all x2 -> x1, starting transfers between devices: 9.18 us -> 11.5 us  [per_device(): got = lax.all_to_all(send, AXES, split_axis=0, concat_axis=2, tiled=True)]
    slice x9 -> x4, local copies, waits for them, and re-layouts: 2.11 us -> 0.06 us  [the longest x1 0.03 us: per_device(): rows_im = jnp.concatenate([zero_row, y_im[:, 1:], zero_row], axis=1)]
    dot_general x4, matrix products: 5.95 us -> 4.43 us  [the longest x2 3 us: per_device(): prod_b = jnp.einsum('akn,nm->akm', both, table_b, precision=highest)]
    transpose x0 -> x1, local copies, waits for them, and re-layouts: none -> 1.19 us  [per_device(): send = jnp.transpose(stacked, (2, 0, 1))]
  transfers between devices with their start and end apart: 2 -> 1, of which waited for: 2 -> 1; matrix products, arithmetic and copies ran while one was open for 1% -> 1% of each run, Pallas kernels for 0% -> 0%
where the time goes in v2:
time: 55.7 us; the launch traced here: 55.5 us
  blocking collectives  17.6 us (32%)
  waiting for transfers between devices  12.8 us (23%)
  starting transfers between devices  11.5 us (21%)
  local copies, waits for them, and re-layouts  4.68 us (8%)
  matrix products  4.43 us (8%)
  other arithmetic  3.51 us (6%)
  between operations  0.92 us (2%)
    all_to_all x1, blocking collectives, per_device(): rows = lax.all_to_all(outs, AXES, split_axis=1, concat_axis=1, tiled=True)  17.6 us
    all_to_all x1, waiting for transfers between devices, per_device(): got = lax.all_to_all(send, AXES, split_axis=0, concat_axis=2, tiled=True)  12.8 us
    all_to_all x1, starting transfers between devices, per_device(): got = lax.all_to_all(send, AXES, split_axis=0, concat_axis=2, tiled=True)  11.5 us
    dot_general x2, matrix products, per_device(): prod_b = jnp.einsum('akn,nm->akm', both, table_b, precision=highest)  3 us
    transpose x1, local copies, waits for them, and re-layouts, per_device(): send = jnp.transpose(stacked, (2, 0, 1))  1.19 us
    transpose x1, other arithmetic, per_device(): send = jnp.transpose(stacked, (2, 0, 1))  1.12 us
  transfers between devices with their start and end apart: 1, of which 1 were waited for; matrix products, arithmetic and copies ran while one was open for 1% of the time, Pallas kernels for 0%

profile of v2, /device:TPU:1, one launch (start us, length us, event | category | flops | bytes accessed | tf_op | source)
XLA Modules:
  0.0 55.5 jit_solution(2330608774567307671)
XLA Ops:
  0.6 0.0 copy-start.3
  0.6 0.0 copy-start.1
  0.7 0.0 copy-start.5
  0.7 1.1 %maximum_bitcast_fusion = bf16[128,3,512]{0,2,1:T(8,128)(2,1)S(1)} fusion(bf16[1,512,128]{2,1,0:T(8,128)(2,1)} %bitcast.32, bf16[1,512,128]{2,1,0:T(8,128)(2,1)} %bitcast.33, bf16[1,512,128]{2,1,0:T(8,128)(2,1)} %bitcast.34), kind=kLoop, calls=%fused_computation.33 | loop fusion | flops 393216 | bytes 786432 | tf_op jit(solution)/shard_map/transpose | solution.py:57
  1.8 1.2 %copy.40 = bf16[128,3,512]{2,1,0:T(4,128)(2,1)} copy(bf16[128,3,512]{0,2,1:T(8,128)(2,1)S(1)} %maximum_bitcast_fusion) | data formatting | bytes 786432 | tf_op jit(solution)/shard_map/transpose | solution.py:57
  3.0 0.0 copy-start.2
  3.0 11.5 %all-to-all-start = ((bf16[128,3,512]{2,1,0:T(4,128)(2,1)}), bf16[128,3,512]{2,1,0:T(4,128)(2,1)S(1)}, u32[]{:S(2)}, u32[]{:S(2)}) async-start(bf16[128,3,512]{2,1,0:T(4,128)(2,1)} %copy.40), calls=%async_computation | async-start | bytes 1048576 | tf_op jit(solution)/shard_map/all_to_all | solution.py:58
  14.5 0.0 copy-done.3
  14.5 0.0 copy-done.1
  14.5 0.0 copy-done.5
  14.6 0.6 %dynamic_slice.4 = f32[1]{0:T(128)} dynamic-slice(f32[128]{0:T(128)S(1)} %copy-done.5, s32[]{:T(128)S(6)} %select_n.4), dynamic_slice_sizes={1} | dynamic-slice | bytes 12 | tf_op jit(solution)/shard_map/jit(dynamic_index_in_dim)/dynamic_slice | solution.py:107
  15.1 12.8 %all-to-all-done = bf16[128,3,512]{2,1,0:T(4,128)(2,1)S(1)} async-done(((bf16[128,3,512]{2,1,0:T(4,128)(2,1)}), bf16[128,3,512]{2,1,0:T(4,128)(2,1)S(1)}, u32[]{:S(2)}, u32[]{:S(2)}) %all-to-all-start) | async-done | bytes 393248 | tf_op jit(solution)/shard_map/all_to_all | solution.py:58
  28.0 0.1 copy.41
  28.0 0.0 copy-start.4
  28.1 0.1 reshape.122
  28.2 0.0 copy-done.2
  28.2 0.5 convolution_bitcast_fusion.1
  28.7 0.0 copy-start
  28.8 0.2 copy-done.4
  29.0 0.1 multiply_subtract_fusion.1
  29.1 0.7 %copy-done = f32[256,512,1]{1,0,2:T(8,128)S(1)} copy-done((f32[256,512,1]{1,0,2:T(8,128)S(1)}, f32[256,512,1]{1,0,2:T(8,128)}, u32[]{:S(2)}) %copy-start) | copy-done | bytes 524312
  29.8 1.5 %fusion = f32[6,129,512]{2,1,0:T(8,128)S(1)} fusion(f32[256,512,1]{1,0,2:T(8,128)S(1)} %copy-done, f32[3,129,256]{2,1,0:T(8,128)S(1)} %get-tuple-element.14, f32[3,129,256]{2,1,0:T(8,128)S(1)} %get-tuple-element.13), kind=kOutput, calls=%fused_computation.2 | convolution fusion | flops 1217594880 | bytes 2902016 | tf_op jit(solution)/shard_map/akn,nm->akm/dot_general | solution.py:72
  31.3 0.1 slice_add_fusion.1
  31.4 0.1 multiply_subtract_fusion.4
  31.5 0.1 multiply_add_fusion.3
  31.5 0.1 maximum_multiply_fusion
  31.6 1.5 %fusion.4 = f32[6,129,512]{2,1,0:T(8,128)S(1)} fusion(f32[256,512,1]{1,0,2:T(8,128)S(1)} %copy-done, f32[3,129,256]{2,1,0:T(8,128)S(1)} %get-tuple-element.29, f32[3,129,256]{2,1,0:T(8,128)S(1)} %get-tuple-element.28), kind=kOutput, calls=%fused_computation.6 | convolution fusion | flops 1217594880 | bytes 2902016 | tf_op jit(solution)/shard_map/akn,nm->akm/dot_general | solution.py:96
  33.1 0.1 multiply_subtract_fusion
  33.3 0.1 convert_element_type.61
  33.4 0.1 fusion.16
  33.5 0.9 %convolution_bitcast_fusion = f32[3,256,256]{2,1,0:T(8,128)S(1)} fusion(f32[256,256,1]{1,0,2:T(8,128)S(1)} %copy-done.2, f32[3,127,256]{2,1,0:T(8,128)S(1)} %fusion.16, f32[3,1,256]{2,1,0:T(1,128)S(1)} %get-tuple-element.25, f32[3,127,256]{2,1,0:T(8,128)S(1)} %slice_multiply_fusion.2, f32[3,1,256]{2,1,0:T(1,128)S(1)} %get-tuple-element.24), kind=kOutput, calls=%fused_computation | convolution fusion | flops 604569600 | bytes 1835008 | tf_op jit(solution)/shard_map/sn,asm->anm/dot_general | solution.py:105
  34.5 0.7 %fusion.21 = (bf16[1,256,256]{2,1,0:T(8,128)(2,1)S(1)}, bf16[1,256,256]{2,1,0:T(8,128)(2,1)S(1)}, f32[1,256,256]{2,1,0:T(8,128)S(1)}) fusion(f32[3,256,256]{2,1,0:T(8,128)S(1)} %convert_element_type.61, f32[3,256,256]{2,1,0:T(8,128)S(1)} %convolution_bitcast_fusion, f32[]{:T(128)} %bitcast.10), kind=kLoop, calls=%fused_computation.42 | loop fusion | flops 393216 | bytes 1835012 | tf_op jit(solution)/shard_map/convert_element_type | solution.py:116
  35.2 0.1 squeeze.11
  35.5 0.1 pad_maximum_fusion
  35.6 0.4 copy.44
  36.0 17.6 %all_to_all.20 = bf16[4,128,512]{2,0,1:T(4,128)(2,1)S(1)} all-to-all(bf16[4,128,512]{2,0,1:T(4,128)(2,1)S(1)} %copy.44), channel_id=1, replica_groups=mesh['seq'=32,'dp'=4] {'seq','dp'}, dimensions={1} | all-to-all | bytes 1048576 | tf_op jit(solution)/shard_map/all_to_all | solution.py:123
  53.6 0.4 copy.45
  54.0 0.7 %slice_bitcast_fusion = (bf16[512,128]{1,0:T(8,128)(2,1)}, bf16[512,128]{1,0:T(8,128)(2,1)}) fusion(bf16[4,512,128]{2,1,0:T(8,128)(2,1)S(1)} %bitcast.30), kind=kLoop, calls=%fused_computation.50 | loop fusion | bytes 524288 | tf_op jit(solution)/shard_map/squeeze | solution.py:126
  54.7 0.7 %add_bitcast_fusion = f32[512,128]{1,0:T(8,128)} fusion(bf16[4,512,128]{2,1,0:T(8,128)(2,1)S(1)} %bitcast.31), kind=kLoop, calls=%fused_computation.43 | loop fusion | flops 196608 | bytes 524288 | tf_op jit(solution)/shard_map/add | solution.py:127
  (9 shorter events, 0.2 us)
Async XLA Ops:
  0.6 13.8 %copy-start.3 = (f32[129,256]{1,0:T(8,128)S(1)}, f32[129,256]{1,0:T(8,128)}, u32[]{:S(2)}) copy-start(f32[129,256]{1,0:T(8,128)} %constant.35) | copy-start | bytes 396292
  0.6 13.9 %copy-start.1 = (f32[129,256]{1,0:T(8,128)S(1)}, f32[129,256]{1,0:T(8,128)}, u32[]{:S(2)}) copy-start(f32[129,256]{1,0:T(8,128)} %constant.32.clone) | copy-start | bytes 396292
  0.7 13.9 %copy-start.5 = (f32[128]{0:T(128)S(1)}, f32[128]{0:T(128)}, u32[]{:S(2)}) copy-start(f32[128]{0:T(128)} %param.10) | copy-start | bytes 1540
  3.0 25.2 %copy-start.2 = (f32[256,256,1]{1,0,2:T(8,128)S(1)}, f32[256,256,1]{1,0,2:T(8,128)}, u32[]{:S(2)}) copy-start(f32[256,256,1]{1,0,2:T(8,128)} %constant.36) | copy-start | bytes 786436
  3.0 25.0 %all-to-all-start = ((bf16[128,3,512]{2,1,0:T(4,128)(2,1)}), bf16[128,3,512]{2,1,0:T(4,128)(2,1)S(1)}, u32[]{:S(2)}, u32[]{:S(2)}) async-start(bf16[128,3,512]{2,1,0:T(4,128)(2,1)} %copy.40), calls=%async_computation | async-start | bytes 1048576 | tf_op jit(solution)/shard_map/all_to_all | solution.py:58
  28.0 0.9 %copy-start.4 = (f32[129,256]{1,0:T(8,128)S(1)}, f32[129,256]{1,0:T(8,128)}, u32[]{:S(2)}) copy-start(f32[129,256]{1,0:T(8,128)} %constant.33.clone) | copy-start | bytes 396292
  28.7 1.1 %copy-start = (f32[256,512,1]{1,0,2:T(8,128)S(1)}, f32[256,512,1]{1,0,2:T(8,128)}, u32[]{:S(2)}) copy-start(f32[256,512,1]{1,0,2:T(8,128)} %constant.37) | copy-start | bytes 1572868

commit v3 on v2

--- a/solution.py
+++ b/solution.py
@@ -9,7 +9,7 @@
 
 AXES = ("seq", "dp")
 
-highest = lax.Precision.HIGHEST
+matmul_precision = lax.Precision.HIGH
 
 
 def half_table(order):
@@ -59,7 +59,7 @@
     seqs = got.reshape(3, side, side).astype(jnp.float32)
 
     table_a = half_table(side)
-    part = jnp.einsum("kn,anm->akm", table_a, seqs, precision=highest)
+    part = jnp.einsum("kn,anm->akm", table_a, seqs, precision=matmul_precision)
     y_re, y_im = part[:, :half], part[:, half:]
     zero_row = jnp.zeros((3, 1, side), jnp.float32)
     rows_re = jnp.concatenate([y_re, y_im[:, 0:1]], axis=1)
@@ -69,7 +69,7 @@
 
     table_b = pair_table(side)
     both = jnp.concatenate([t_re, t_im], axis=0)
-    prod_b = jnp.einsum("akn,nm->akm", both, table_b, precision=highest)
+    prod_b = jnp.einsum("akn,nm->akm", both, table_b, precision=matmul_precision)
     cc, cs = prod_b[..., :side], prod_b[..., side:]
     s_re = cc[:3] + cs[3:]
     s_im = cc[3:] - cs[:3]
@@ -93,7 +93,7 @@
     ) * scale
 
     both = jnp.concatenate([p_re, p_im], axis=0)
-    prod_b = jnp.einsum("akn,nm->akm", both, table_b, precision=highest)
+    prod_b = jnp.einsum("akn,nm->akm", both, table_b, precision=matmul_precision)
     cc, cs = prod_b[..., :side], prod_b[..., side:]
     u_re = cc[:3] - cs[3:]
     u_im = cc[3:] + cs[:3]
@@ -102,7 +102,7 @@
     pack_re = jnp.concatenate([v_re[:, 0:1], 2.0 * v_re[:, 1:half]], axis=1)
     pack_im = jnp.concatenate([v_re[:, half:], 2.0 * v_im[:, 1:half]], axis=1)
     packed = jnp.concatenate([pack_re, pack_im], axis=1)
-    times = jnp.einsum("sn,asm->anm", table_a, packed, precision=highest).reshape(3, length)
+    times = jnp.einsum("sn,asm->anm", table_a, packed, precision=matmul_precision).reshape(3, length)
 
     gain = lax.dynamic_index_in_dim(skip_gain, me, keepdims=False)
     flat = seqs.reshape(3, length)

time: 55.7 us -> 53.9 us (0.968)
  matrix products: 4.43 us -> 2.61 us
    dot_general x4, matrix products: 4.43 us -> 2.61 us  [the longest x2 1.66 us: per_device(): jnp.einsum('akn,nm->akm', both, table_b, precision=matmul_precision)]
where the time goes in v3:
time: 53.9 us; the launch traced here: 53.6 us
  blocking collectives  17.6 us (33%)
  waiting for transfers between devices  12.8 us (24%)
  starting transfers between devices  11.5 us (21%)
  local copies, waits for them, and re-layouts  4.68 us (9%)
  other arithmetic  3.51 us (7%)
  matrix products  2.61 us (5%)
  between operations  0.92 us (2%)
    all_to_all x1, blocking collectives, per_device(): rows = lax.all_to_all(outs, AXES, split_axis=1, concat_axis=1, tiled=True)  17.6 us
    all_to_all x1, waiting for transfers between devices, per_device(): got = lax.all_to_all(send, AXES, split_axis=0, concat_axis=2, tiled=True)  12.8 us
    all_to_all x1, starting transfers between devices, per_device(): got = lax.all_to_all(send, AXES, split_axis=0, concat_axis=2, tiled=True)  11.5 us
    dot_general x2, matrix products, per_device(): jnp.einsum('akn,nm->akm', both, table_b, precision=matmul_precision)  1.66 us
    transpose x1, local copies, waits for them, and re-layouts, per_device(): send = jnp.transpose(stacked, (2, 0, 1))  1.19 us
    transpose x1, other arithmetic, per_device(): send = jnp.transpose(stacked, (2, 0, 1))  1.12 us
  transfers between devices with their start and end apart: 1, of which 1 were waited for; matrix products, arithmetic and copies ran while one was open for 1% of the time, Pallas kernels for 0%

profile of v3, /device:TPU:1, one launch (start us, length us, event | category | flops | bytes accessed | tf_op | source)
XLA Modules:
  0.0 53.6 jit_solution(13398599424850496347)
XLA Ops:
  0.6 0.0 copy-start.3
  0.6 0.0 copy-start.1
  0.7 0.0 copy-start.5
  0.7 1.1 %maximum_bitcast_fusion = bf16[128,3,512]{0,2,1:T(8,128)(2,1)S(1)} fusion(bf16[1,512,128]{2,1,0:T(8,128)(2,1)} %bitcast.32, bf16[1,512,128]{2,1,0:T(8,128)(2,1)} %bitcast.33, bf16[1,512,128]{2,1,0:T(8,128)(2,1)} %bitcast.34), kind=kLoop, calls=%fused_computation.33 | loop fusion | flops 393216 | bytes 786432 | tf_op jit(solution)/shard_map/transpose | solution.py:57
  1.8 1.2 %copy.40 = bf16[128,3,512]{2,1,0:T(4,128)(2,1)} copy(bf16[128,3,512]{0,2,1:T(8,128)(2,1)S(1)} %maximum_bitcast_fusion) | data formatting | bytes 786432 | tf_op jit(solution)/shard_map/transpose | solution.py:57
  3.0 0.0 copy-start.2
  3.0 11.5 %all-to-all-start = ((bf16[128,3,512]{2,1,0:T(4,128)(2,1)}), bf16[128,3,512]{2,1,0:T(4,128)(2,1)S(1)}, u32[]{:S(2)}, u32[]{:S(2)}) async-start(bf16[128,3,512]{2,1,0:T(4,128)(2,1)} %copy.40), calls=%async_computation | async-start | bytes 1048576 | tf_op jit(solution)/shard_map/all_to_all | solution.py:58
  14.5 0.0 copy-done.3
  14.5 0.0 copy-done.1
  14.5 0.0 copy-done.5
  14.6 0.6 %dynamic_slice.4 = f32[1]{0:T(128)} dynamic-slice(f32[128]{0:T(128)S(1)} %copy-done.5, s32[]{:T(128)S(6)} %select_n.4), dynamic_slice_sizes={1} | dynamic-slice | bytes 12 | tf_op jit(solution)/shard_map/jit(dynamic_index_in_dim)/dynamic_slice | solution.py:107
  15.1 12.8 %all-to-all-done = bf16[128,3,512]{2,1,0:T(4,128)(2,1)S(1)} async-done(((bf16[128,3,512]{2,1,0:T(4,128)(2,1)}), bf16[128,3,512]{2,1,0:T(4,128)(2,1)S(1)}, u32[]{:S(2)}, u32[]{:S(2)}) %all-to-all-start) | async-done | bytes 393248 | tf_op jit(solution)/shard_map/all_to_all | solution.py:58
  28.0 0.1 copy.41
  28.0 0.0 copy-start.4
  28.1 0.1 reshape.122
  28.2 0.0 copy-done.2
  28.2 0.4 convolution_bitcast_fusion.1
  28.6 0.0 copy-start
  28.7 0.3 copy-done.4
  29.0 0.1 multiply_subtract_fusion.1
  29.1 0.6 %copy-done = f32[256,512,1]{1,0,2:T(8,128)S(1)} copy-done((f32[256,512,1]{1,0,2:T(8,128)S(1)}, f32[256,512,1]{1,0,2:T(8,128)}, u32[]{:S(2)}) %copy-start) | copy-done | bytes 524312
  29.7 0.8 %fusion = f32[6,129,512]{2,1,0:T(8,128)S(1)} fusion(f32[256,512,1]{1,0,2:T(8,128)S(1)} %copy-done, f32[3,129,256]{2,1,0:T(8,128)S(1)} %get-tuple-element.14, f32[3,129,256]{2,1,0:T(8,128)S(1)} %get-tuple-element.13), kind=kOutput, calls=%fused_computation.2 | convolution fusion | flops 608896512 | bytes 2902016 | tf_op jit(solution)/shard_map/akn,nm->akm/dot_general | solution.py:72
  30.5 0.1 slice_add_fusion.1
  30.6 0.1 multiply_subtract_fusion.4
  30.7 0.1 multiply_add_fusion.3
  30.8 0.1 maximum_multiply_fusion
  30.8 0.8 %fusion.4 = f32[6,129,512]{2,1,0:T(8,128)S(1)} fusion(f32[256,512,1]{1,0,2:T(8,128)S(1)} %copy-done, f32[3,129,256]{2,1,0:T(8,128)S(1)} %get-tuple-element.29, f32[3,129,256]{2,1,0:T(8,128)S(1)} %get-tuple-element.28), kind=kOutput, calls=%fused_computation.6 | convolution fusion | flops 608896512 | bytes 2902016 | tf_op jit(solution)/shard_map/akn,nm->akm/dot_general | solution.py:96
  31.7 0.1 multiply_subtract_fusion
  31.9 0.1 convert_element_type.61
  32.0 0.1 fusion.16
  32.1 0.6 %convolution_bitcast_fusion = f32[3,256,256]{2,1,0:T(8,128)S(1)} fusion(f32[256,256,1]{1,0,2:T(8,128)S(1)} %copy-done.2, f32[3,127,256]{2,1,0:T(8,128)S(1)} %fusion.16, f32[3,1,256]{2,1,0:T(1,128)S(1)} %get-tuple-element.25, f32[3,127,256]{2,1,0:T(8,128)S(1)} %slice_multiply_fusion.2, f32[3,1,256]{2,1,0:T(1,128)S(1)} %get-tuple-element.24), kind=kOutput, calls=%fused_computation | convolution fusion | flops 302579712 | bytes 1835008 | tf_op jit(solution)/shard_map/sn,asm->anm/dot_general | solution.py:105
  32.7 0.7 %fusion.21 = (bf16[1,256,256]{2,1,0:T(8,128)(2,1)S(1)}, bf16[1,256,256]{2,1,0:T(8,128)(2,1)S(1)}, f32[1,256,256]{2,1,0:T(8,128)S(1)}) fusion(f32[3,256,256]{2,1,0:T(8,128)S(1)} %convert_element_type.61, f32[3,256,256]{2,1,0:T(8,128)S(1)} %convolution_bitcast_fusion, f32[]{:T(128)} %bitcast.10), kind=kLoop, calls=%fused_computation.42 | loop fusion | flops 393216 | bytes 1835012 | tf_op jit(solution)/shard_map/convert_element_type | solution.py:116
  33.4 0.1 squeeze.11
  33.7 0.1 pad_maximum_fusion
  33.7 0.4 copy.44
  34.1 17.6 %all_to_all.20 = bf16[4,128,512]{2,0,1:T(4,128)(2,1)S(1)} all-to-all(bf16[4,128,512]{2,0,1:T(4,128)(2,1)S(1)} %copy.44), channel_id=1, replica_groups=mesh['seq'=32,'dp'=4] {'seq','dp'}, dimensions={1} | all-to-all | bytes 1048576 | tf_op jit(solution)/shard_map/all_to_all | solution.py:123
  51.8 0.4 copy.45
  52.2 0.7 %slice_bitcast_fusion = (bf16[512,128]{1,0:T(8,128)(2,1)}, bf16[512,128]{1,0:T(8,128)(2,1)}) fusion(bf16[4,512,128]{2,1,0:T(8,128)(2,1)S(1)} %bitcast.30), kind=kLoop, calls=%fused_computation.50 | loop fusion | bytes 524288 | tf_op jit(solution)/shard_map/squeeze | solution.py:126
  52.9 0.7 %add_bitcast_fusion = f32[512,128]{1,0:T(8,128)} fusion(bf16[4,512,128]{2,1,0:T(8,128)(2,1)S(1)} %bitcast.31), kind=kLoop, calls=%fused_computation.43 | loop fusion | flops 196608 | bytes 524288 | tf_op jit(solution)/shard_map/add | solution.py:127
  (9 shorter events, 0.2 us)
Async XLA Ops:
  0.6 13.8 %copy-start.3 = (f32[129,256]{1,0:T(8,128)S(1)}, f32[129,256]{1,0:T(8,128)}, u32[]{:S(2)}) copy-start(f32[129,256]{1,0:T(8,128)} %constant.35) | copy-start | bytes 396292
  0.6 13.9 %copy-start.1 = (f32[129,256]{1,0:T(8,128)S(1)}, f32[129,256]{1,0:T(8,128)}, u32[]{:S(2)}) copy-start(f32[129,256]{1,0:T(8,128)} %constant.32.clone) | copy-start | bytes 396292
  0.7 13.9 %copy-start.5 = (f32[128]{0:T(128)S(1)}, f32[128]{0:T(128)}, u32[]{:S(2)}) copy-start(f32[128]{0:T(128)} %param.10) | copy-start | bytes 1540
  3.0 25.2 %copy-start.2 = (f32[256,256,1]{1,0,2:T(8,128)S(1)}, f32[256,256,1]{1,0,2:T(8,128)}, u32[]{:S(2)}) copy-start(f32[256,256,1]{1,0,2:T(8,128)} %constant.36) | copy-start | bytes 786436
  3.0 25.0 %all-to-all-start = ((bf16[128,3,512]{2,1,0:T(4,128)(2,1)}), bf16[128,3,512]{2,1,0:T(4,128)(2,1)S(1)}, u32[]{:S(2)}, u32[]{:S(2)}) async-start(bf16[128,3,512]{2,1,0:T(4,128)(2,1)} %copy.40), calls=%async_computation | async-start | bytes 1048576 | tf_op jit(solution)/shard_map/all_to_all | solution.py:58
  28.0 0.9 %copy-start.4 = (f32[129,256]{1,0:T(8,128)S(1)}, f32[129,256]{1,0:T(8,128)}, u32[]{:S(2)}) copy-start(f32[129,256]{1,0:T(8,128)} %constant.33.clone) | copy-start | bytes 396292
  28.6 1.1 %copy-start = (f32[256,512,1]{1,0,2:T(8,128)S(1)}, f32[256,512,1]{1,0,2:T(8,128)}, u32[]{:S(2)}) copy-start(f32[256,512,1]{1,0,2:T(8,128)} %constant.37) | copy-start | bytes 1572868

commit v4 on v3

--- a/solution.py
+++ b/solution.py
@@ -54,8 +54,9 @@
     assert chans == dev_count and side * side == length
 
     stacked = jnp.stack([signal, out_grad, filter_param], axis=0)
-    send = jnp.transpose(stacked, (2, 0, 1))
-    got = lax.all_to_all(send, AXES, split_axis=0, concat_axis=2, tiled=True)
+    send = jnp.transpose(stacked, (2, 0, 1)).reshape(dev_count, 4, 3 * tok_rows // 4)
+    got = lax.all_to_all(send, AXES, split_axis=0, concat_axis=0, tiled=True)
+    got = jnp.transpose(got.reshape(dev_count, 3, tok_rows), (1, 0, 2))
     seqs = got.reshape(3, side, side).astype(jnp.float32)
 
     table_a = half_table(side)

time: 53.9 us -> 52.8 us (0.980)
  waiting for transfers between devices: 12.8 us -> 11.6 us
    all_to_all x1, waiting for transfers between devices: 12.8 us -> 11.6 us  [per_device(): got = lax.all_to_all(send, AXES, split_axis=0, concat_axis=0, tiled=True)]
    another operation x0 -> x1, other arithmetic: none -> 1.12 us  [per_device(): stacked = jnp.stack([signal, out_grad, filter_param], axis=0)]
    transpose x1 -> x0, other arithmetic: 1.12 us -> none  [per_device(): send = jnp.transpose(stacked, (2, 0, 1))]
    transpose x1, local copies, waits for them, and re-layouts: 1.19 us -> 0.18 us  [per_device(): got = jnp.transpose(got.reshape(dev_count, 3, tok_rows), (1, 0, 2))]
    reshape x0 -> x1, local copies, waits for them, and re-layouts: none -> 0.97 us  [per_device(): jnp.transpose(stacked, (2, 0, 1)).reshape(dev_count, 4, 3 * tok_rows // 4)]
where the time goes in v4:
time: 52.8 us; the launch traced here: 52.6 us
  blocking collectives  17.6 us (33%)
  waiting for transfers between devices  11.6 us (22%)
  starting transfers between devices  11.5 us (22%)
  local copies, waits for them, and re-layouts  4.86 us (9%)
  other arithmetic  3.51 us (7%)
  matrix products  2.6 us (5%)
  between operations  0.93 us (2%)
    all_to_all x1, blocking collectives, per_device(): rows = lax.all_to_all(outs, AXES, split_axis=1, concat_axis=1, tiled=True)  17.6 us
    all_to_all x1, waiting for transfers between devices, per_device(): got = lax.all_to_all(send, AXES, split_axis=0, concat_axis=0, tiled=True)  11.6 us
    all_to_all x1, starting transfers between devices, per_device(): got = lax.all_to_all(send, AXES, split_axis=0, concat_axis=0, tiled=True)  11.5 us
    dot_general x2, matrix products, per_device(): jnp.einsum('akn,nm->akm', both, table_b, precision=matmul_precision)  1.66 us
    another operation x1, other arithmetic, per_device(): stacked = jnp.stack([signal, out_grad, filter_param], axis=0)  1.12 us
  transfers between devices with their start and end apart: 1, of which 1 were waited for; matrix products, arithmetic and copies ran while one was open for 1% of the time, Pallas kernels for 0%

profile of v4, /device:TPU:1, one launch (start us, length us, event | category | flops | bytes accessed | tf_op | source)
XLA Modules:
  0.0 52.6 jit_solution(9498442281245619426)
XLA Ops:
  0.6 0.0 copy-start.3
  0.6 0.0 copy-start.1
  0.7 0.0 copy-start.5
  0.7 1.1 %pad_maximum_fusion.2 = bf16[3,512,128]{2,1,0:T(8,128)(2,1)S(1)} fusion(bf16[1,512,128]{2,1,0:T(8,128)(2,1)} %bitcast.32, bf16[1,512,128]{2,1,0:T(8,128)(2,1)} %bitcast.33, bf16[1,512,128]{2,1,0:T(8,128)(2,1)} %bitcast.34), kind=kLoop, calls=%fused_computation.33 | loop fusion | flops 393216 | bytes 786432 | tf_op jit(solution)/shard_map/stack | solution.py:56
  1.8 1.0 %copy.46 = bf16[128,4,384]{2,1,0:T(4,128)(2,1)} copy(bf16[128,4,384]{0,2,1:T(8,128)(2,1)S(1)} %bitcast.31) | data formatting | bytes 786432 | tf_op jit(solution)/shard_map/reshape | solution.py:57
  2.8 0.0 copy-start.2
  2.8 11.5 %all-to-all-start = ((bf16[128,4,384]{2,1,0:T(4,128)(2,1)}), bf16[128,4,384]{2,1,0:T(4,128)(2,1)S(1)}, u32[]{:S(2)}, u32[]{:S(2)}) async-start(bf16[128,4,384]{2,1,0:T(4,128)(2,1)} %copy.46), calls=%async_computation | async-start | bytes 786432 | tf_op jit(solution)/shard_map/all_to_all | solution.py:58
  14.3 0.0 copy-done.3
  14.3 0.0 copy-done.1
  14.3 0.0 copy-done.5
  14.3 0.6 %dynamic_slice.4 = f32[1]{0:T(128)} dynamic-slice(f32[128]{0:T(128)S(1)} %copy-done.5, s32[]{:T(128)S(6)} %select_n.4), dynamic_slice_sizes={1} | dynamic-slice | bytes 12 | tf_op jit(solution)/shard_map/jit(dynamic_index_in_dim)/dynamic_slice | solution.py:108
  14.9 11.6 %all-to-all-done = bf16[128,4,384]{2,1,0:T(4,128)(2,1)S(1)} async-done(((bf16[128,4,384]{2,1,0:T(4,128)(2,1)}), bf16[128,4,384]{2,1,0:T(4,128)(2,1)S(1)}, u32[]{:S(2)}, u32[]{:S(2)}) %all-to-all-start) | async-done | bytes 393248 | tf_op jit(solution)/shard_map/all_to_all | solution.py:58
  26.5 0.3 copy.47
  26.8 0.2 copy.48
  27.0 0.0 copy-start.4
  27.0 0.1 reshape.129
  27.2 0.0 copy-done.2
  27.2 0.4 convolution_bitcast_fusion.1
  27.5 0.0 copy-start
  27.6 0.3 copy-done.4
  27.9 0.1 multiply_subtract_fusion.1
  28.0 0.6 %copy-done = f32[256,512,1]{1,0,2:T(8,128)S(1)} copy-done((f32[256,512,1]{1,0,2:T(8,128)S(1)}, f32[256,512,1]{1,0,2:T(8,128)}, u32[]{:S(2)}) %copy-start) | copy-done | bytes 524312
  28.6 0.8 %fusion = f32[6,129,512]{2,1,0:T(8,128)S(1)} fusion(f32[256,512,1]{1,0,2:T(8,128)S(1)} %copy-done, f32[3,129,256]{2,1,0:T(8,128)S(1)} %get-tuple-element.14, f32[3,129,256]{2,1,0:T(8,128)S(1)} %get-tuple-element.13), kind=kOutput, calls=%fused_computation.2 | convolution fusion | flops 608896512 | bytes 2902016 | tf_op jit(solution)/shard_map/akn,nm->akm/dot_general | solution.py:73
  29.4 0.1 slice_add_fusion.1
  29.6 0.1 multiply_subtract_fusion.4
  29.7 0.1 multiply_add_fusion.3
  29.7 0.1 maximum_multiply_fusion
  29.8 0.8 %fusion.4 = f32[6,129,512]{2,1,0:T(8,128)S(1)} fusion(f32[256,512,1]{1,0,2:T(8,128)S(1)} %copy-done, f32[3,129,256]{2,1,0:T(8,128)S(1)} %get-tuple-element.29, f32[3,129,256]{2,1,0:T(8,128)S(1)} %get-tuple-element.28), kind=kOutput, calls=%fused_computation.6 | convolution fusion | flops 608896512 | bytes 2902016 | tf_op jit(solution)/shard_map/akn,nm->akm/dot_general | solution.py:97
  30.6 0.1 multiply_subtract_fusion
  30.9 0.1 convert_element_type.61
  30.9 0.1 fusion.16
  31.0 0.6 %convolution_bitcast_fusion = f32[3,256,256]{2,1,0:T(8,128)S(1)} fusion(f32[256,256,1]{1,0,2:T(8,128)S(1)} %copy-done.2, f32[3,127,256]{2,1,0:T(8,128)S(1)} %fusion.16, f32[3,1,256]{2,1,0:T(1,128)S(1)} %get-tuple-element.25, f32[3,127,256]{2,1,0:T(8,128)S(1)} %slice_multiply_fusion.2, f32[3,1,256]{2,1,0:T(1,128)S(1)} %get-tuple-element.24), kind=kOutput, calls=%fused_computation | convolution fusion | flops 302579712 | bytes 1835008 | tf_op jit(solution)/shard_map/sn,asm->anm/dot_general | solution.py:106
  31.6 0.7 %fusion.21 = (bf16[1,256,256]{2,1,0:T(8,128)(2,1)S(1)}, bf16[1,256,256]{2,1,0:T(8,128)(2,1)S(1)}, f32[1,256,256]{2,1,0:T(8,128)S(1)}) fusion(f32[3,256,256]{2,1,0:T(8,128)S(1)} %convert_element_type.61, f32[3,256,256]{2,1,0:T(8,128)S(1)} %convolution_bitcast_fusion, f32[]{:T(128)} %bitcast.11), kind=kLoop, calls=%fused_computation.42 | loop fusion | flops 393216 | bytes 1835012 | tf_op jit(solution)/shard_map/convert_element_type | solution.py:117
  32.4 0.1 squeeze.11
  32.6 0.1 pad_maximum_fusion
  32.7 0.4 copy.51
  33.1 17.6 %all_to_all.10 = bf16[4,128,512]{2,0,1:T(4,128)(2,1)S(1)} all-to-all(bf16[4,128,512]{2,0,1:T(4,128)(2,1)S(1)} %copy.51), channel_id=1, replica_groups=mesh['seq'=32,'dp'=4] {'seq','dp'}, dimensions={1} | all-to-all | bytes 1048576 | tf_op jit(solution)/shard_map/all_to_all | solution.py:124
  50.7 0.4 copy.52
  51.1 0.7 %slice_bitcast_fusion = (bf16[512,128]{1,0:T(8,128)(2,1)}, bf16[512,128]{1,0:T(8,128)(2,1)}) fusion(bf16[4,512,128]{2,1,0:T(8,128)(2,1)S(1)} %bitcast.28), kind=kLoop, calls=%fused_computation.50 | loop fusion | bytes 524288 | tf_op jit(solution)/shard_map/squeeze | solution.py:127
  51.8 0.7 %add_bitcast_fusion = f32[512,128]{1,0:T(8,128)} fusion(bf16[4,512,128]{2,1,0:T(8,128)(2,1)S(1)} %bitcast.29), kind=kLoop, calls=%fused_computation.43 | loop fusion | flops 196608 | bytes 524288 | tf_op jit(solution)/shard_map/add | solution.py:128
  (9 shorter events, 0.2 us)
Async XLA Ops:
  0.6 13.6 %copy-start.3 = (f32[129,256]{1,0:T(8,128)S(1)}, f32[129,256]{1,0:T(8,128)}, u32[]{:S(2)}) copy-start(f32[129,256]{1,0:T(8,128)} %constant.35) | copy-start | bytes 396292
  0.6 13.6 %copy-start.1 = (f32[129,256]{1,0:T(8,128)S(1)}, f32[129,256]{1,0:T(8,128)}, u32[]{:S(2)}) copy-start(f32[129,256]{1,0:T(8,128)} %constant.32.clone) | copy-start | bytes 396292
  0.7 13.7 %copy-start.5 = (f32[128]{0:T(128)S(1)}, f32[128]{0:T(128)}, u32[]{:S(2)}) copy-start(f32[128]{0:T(128)} %param.10) | copy-start | bytes 1540
  2.8 24.4 %copy-start.2 = (f32[256,256,1]{1,0,2:T(8,128)S(1)}, f32[256,256,1]{1,0,2:T(8,128)}, u32[]{:S(2)}) copy-start(f32[256,256,1]{1,0,2:T(8,128)} %constant.36) | copy-start | bytes 786436
  2.8 23.7 %all-to-all-start = ((bf16[128,4,384]{2,1,0:T(4,128)(2,1)}), bf16[128,4,384]{2,1,0:T(4,128)(2,1)S(1)}, u32[]{:S(2)}, u32[]{:S(2)}) async-start(bf16[128,4,384]{2,1,0:T(4,128)(2,1)} %copy.46), calls=%async_computation | async-start | bytes 786432 | tf_op jit(solution)/shard_map/all_to_all | solution.py:58
  27.0 0.9 %copy-start.4 = (f32[129,256]{1,0:T(8,128)S(1)}, f32[129,256]{1,0:T(8,128)}, u32[]{:S(2)}) copy-start(f32[129,256]{1,0:T(8,128)} %constant.33.clone) | copy-start | bytes 396292
  27.5 1.1 %copy-start = (f32[256,512,1]{1,0,2:T(8,128)S(1)}, f32[256,512,1]{1,0,2:T(8,128)}, u32[]{:S(2)}) copy-start(f32[256,512,1]{1,0,2:T(8,128)} %constant.37) | copy-start | bytes 1572868
